TPU v7x, 256 devices: a whole 4x4x8 slice. The times are simulated.
256 devices in a mesh: clip: 4 (over z_hi, core), fsdp: 64 (over y, z_lo, x).
Axes of the slice: x: 4, y: 4, z: 8 (z_hi: 2, z_lo: 4; z = z_hi * 4 + z_lo), core: 2. Of those that a mesh axis runs over, the one named last changes fastest.
Arguments:
- span_queries: bfloat16 [64, 512, 2560], P('fsdp', None, 'clip'), may hold values from -20 to 20
- span_keys: bfloat16 [64, 512, 2560], P('fsdp', None, 'clip'), may hold values from -12 to 12
- span_values: bfloat16 [64, 512, 2560], P('fsdp', None, 'clip'), may hold values from -6 to 6
- cache_keys: bfloat16 [128, 512, 2560], P(None, 'fsdp', 'clip'), may hold values from -6 to 6
- cache_values: bfloat16 [128, 512, 2560], P(None, 'fsdp', 'clip'), may hold values from -6 to 6
- page_table: int32 [128], replicated, may hold values from 0 to 127, each once
- frame_lists: int32 [64, 6], replicated, may hold values from 0 to 15, as said below
- list_counts: int32 [64], replicated, may hold values from 1 to 6, as said below
- out_weight: bfloat16 [2560, 5120], P('clip', 'fsdp'), may hold values from -1 to 1
Outputs:
- projected: bfloat16 [64, 512, 5120], P('fsdp', 'clip')
Inputs may be any that keep to these rules, and one draw needn't show every extreme that they name: `frame_lists`: each row holds 6 different cached frames; a frame attends to the first list_counts of them. `list_counts`: the counts of frames 2 * i and 2 * i + 1 sum to exactly 7; some frame attends to exactly 6. `page_table`: every block number once.
All inputs are finite; a program needn't handle non-finite values.
Results may differ from a plain program's by a relative error of at most 0.017.
Values may be sent and summed in bfloat16 or wider, within the bound.
No kernel may reach another device: no remote copies, remote signals or barrier semaphores. Data moves between devices by JAX's collectives and lax.ppermute only.
A program may use at most 128 MiB of HBM per device.

v0:
```python
import math
import jax
import jax.numpy as jnp
from jax import lax
from jax.sharding import PartitionSpec as P

HD = 128
CF = 8
NC = 16
neg_fill = -1e30


def lookup(values_table, positions):
    table_width = values_table.shape[0]
    matches = positions[..., None] == jnp.arange(table_width, dtype=jnp.int32)
    return jnp.sum(jnp.where(matches, values_table, 0), axis=-1)


def block_numbers(frame_index, slot_index, page_table, frame_lists):
    max_slots = frame_lists.shape[1]
    listed = lookup(frame_lists.reshape(-1), frame_index * max_slots + slot_index)
    return lookup(page_table, frame_index // CF * NC + listed)


def pick_blocks(send_blocks, cache_keys, cache_values):
    slot_total = send_blocks.shape[0]
    frames = send_blocks.shape[1]
    token_slice = cache_keys.shape[1]
    row_width = cache_keys.shape[2]
    sent_keys = cache_keys[send_blocks].reshape(slot_total, frames * token_slice, row_width)
    sent_values = cache_values[send_blocks].reshape(slot_total, frames * token_slice, row_width)
    return (sent_keys, sent_values)


def empty_state(tokens_here, heads_here):
    return (
        jnp.full((tokens_here, heads_here), neg_fill, jnp.float32),
        jnp.zeros((tokens_here, heads_here), jnp.float32),
        jnp.zeros((tokens_here, heads_here, HD), jnp.float32),
    )


def absorb(carried, query_block, key_block, value_block):
    running_max, running_sum, running_out = carried
    scores = jnp.einsum(
        "qhd,khd->qhk", query_block, key_block, preferred_element_type=jnp.float32
    ) * (1.0 / math.sqrt(HD))
    new_max = jnp.maximum(running_max, jnp.max(scores, axis=2))
    shrink = jnp.exp(running_max - new_max)
    weights = jnp.exp(scores - new_max[:, :, None])
    running_sum = running_sum * shrink + jnp.sum(weights, axis=2)
    running_out = running_out * shrink[:, :, None] + jnp.einsum(
        "qhk,khd->qhd",
        weights.astype(jnp.bfloat16),
        value_block,
        preferred_element_type=jnp.float32,
    )
    return (new_max, running_sum, running_out)


def local(
    span_queries,
    span_keys,
    span_values,
    cache_keys,
    cache_values,
    page_table,
    frame_lists,
    list_counts,
    out_weight,
):
    frames = lax.axis_size("fsdp")
    own_frame = lax.axis_index("fsdp")
    tokens_here = span_queries.shape[1]
    row_width = span_queries.shape[2]
    heads_here = row_width // HD
    max_slots = frame_lists.shape[1]
    own_queries = span_queries[0].reshape(tokens_here, heads_here, HD)
    own_keys = span_keys[0].reshape(tokens_here, heads_here, HD)
    own_values = span_values[0].reshape(tokens_here, heads_here, HD)
    destinations = jnp.arange(frames, dtype=jnp.int32)[:, None]
    blank = empty_state(tokens_here, heads_here)
    started = absorb(blank, own_queries, own_keys, own_values)
    slot_index = jnp.arange(max_slots, dtype=jnp.int32)[None, :]
    send_blocks = block_numbers(destinations, slot_index, page_table, frame_lists).T
    sent_keys, sent_values = pick_blocks(send_blocks, cache_keys, cache_values)
    arrived_keys, arrived_values = (
        lax.all_to_all(sent_keys, "fsdp", split_axis=1, concat_axis=1, tiled=True),
        lax.all_to_all(sent_values, "fsdp", split_axis=1, concat_axis=1, tiled=True),
    )
    arrived_keys = arrived_keys.reshape(max_slots, tokens_here, heads_here, HD)
    arrived_values = arrived_values.reshape(max_slots, tokens_here, heads_here, HD)
    item_count = lookup(list_counts, own_frame)

    def advance_own(item_number, carried_one):
        return absorb(
            carried_one, own_queries, arrived_keys[item_number], arrived_values[item_number]
        )

    final_state = lax.fori_loop(0, item_count, advance_own, started)
    running_sum = final_state[1]
    running_out = final_state[2]
    attended = (
        (running_out / running_sum[:, :, None]).astype(jnp.bfloat16).reshape(tokens_here, row_width)
    )
    partial_value = jnp.dot(
        attended,
        lax.all_gather(out_weight, "fsdp", axis=1, tiled=True),
        preferred_element_type=jnp.float32,
    )
    own_rows = lax.psum_scatter(
        partial_value.astype(jnp.bfloat16), "clip", scatter_dimension=0, tiled=True
    )
    return own_rows[None]


def solution(mesh):
    in_specs = (
        P("fsdp", None, "clip"),
        P("fsdp", None, "clip"),
        P("fsdp", None, "clip"),
        P(None, "fsdp", "clip"),
        P(None, "fsdp", "clip"),
        P(),
        P(),
        P(),
        P("clip", "fsdp"),
    )
    out_specs = P("fsdp", "clip", None)
    return jax.shard_map(local, mesh=mesh, in_specs=in_specs, out_specs=out_specs, check_vma=False)
```

profile of v0, /device:TPU:1, one launch (start us, length us, event | category | flops | bytes accessed | tf_op | source)
XLA Modules:
  0.0 632.7 jit_solution(13444650917698095707)
XLA Ops:
  6.5 0.0 copy-start
  6.5 0.9 copy.82
  7.4 0.1 reshape.110
  7.6 0.3 select_reduce_fusion
  7.9 0.9 select_reduce_fusion.1
  8.8 0.1 reshape.118
  8.9 0.0 copy-done
  8.9 3.6 gather_fusion
  12.5 6.8 %copy.83 = bf16[6,512,640]{2,0,1:T(8,128)(2,1)} copy(bf16[6,512,640]{2,1,0:T(8,128)(2,1)} %bitcast.77) | data formatting | bytes 7864320 | tf_op jit(solution)/shard_map/reshape | solution.py:30
  19.3 0.0 copy-start.2
  19.3 12.9 %all-to-all-start = ((bf16[6,512,640]{2,0,1:T(8,128)(2,1)}), bf16[6,512,640]{2,0,1:T(8,128)(2,1)}, u32[]{:S(2)}, u32[]{:S(2)}) async-start(bf16[6,512,640]{2,0,1:T(8,128)(2,1)} %copy.83), calls=%async_computation | async-start | bytes 10485760 | tf_op jit(solution)/shard_map/all_to_all | solution.py:88
  32.2 0.0 copy-done.2
  32.2 3.5 gather_fusion.1
  35.7 6.8 %copy.85 = bf16[6,512,640]{2,0,1:T(8,128)(2,1)} copy(bf16[6,512,640]{2,1,0:T(8,128)(2,1)} %bitcast.76) | data formatting | bytes 7864320 | tf_op jit(solution)/shard_map/reshape | solution.py:31
  42.5 0.0 copy-start.3
  42.5 0.0 copy-start.4
  42.5 0.0 copy-start.5
  42.5 105.9 %all-to-all-done = bf16[6,512,640]{2,0,1:T(8,128)(2,1)} async-done(((bf16[6,512,640]{2,0,1:T(8,128)(2,1)}), bf16[6,512,640]{2,0,1:T(8,128)(2,1)}, u32[]{:S(2)}, u32[]{:S(2)}) %all-to-all-start) | async-done | bytes 3932192 | tf_op jit(solution)/shard_map/all_to_all | solution.py:88
  148.4 8.5 %all-to-all-start.1 = ((bf16[6,512,640]{2,0,1:T(8,128)(2,1)}), bf16[6,512,640]{2,0,1:T(8,128)(2,1)}, u32[]{:S(2)}, u32[]{:S(2)}) async-start(bf16[6,512,640]{2,0,1:T(8,128)(2,1)} %copy.85), calls=%async_computation.1 | async-start | bytes 10485760 | tf_op jit(solution)/shard_map/all_to_all | solution.py:89
  156.9 0.0 all-gather.2.cloned.1.call-start
  156.9 0.7 all-gather.2.cloned.1.call-update
  157.6 0.2 reduce-scatter.2.cloned.1.call-start
  157.9 0.0 copy-done.3
  157.9 0.3 copy.76
  158.1 0.0 copy-done.4
  158.1 0.3 copy.75
  158.4 0.0 copy-done.5
  158.4 0.3 copy.79
  158.7 0.3 copy.89
  159.0 0.9 bitcast_reduce_fusion.1
  159.9 0.9 fusion.23
  160.8 0.0 copy-start.6
  160.8 2.5 fusion.31
  163.4 1.7 copy.87
  165.1 0.0 copy-done.6
  165.1 0.7 fusion.35
  165.8 8.1 %copy.84 = bf16[6,512,640]{1,2,0:T(8,128)(2,1)} copy(bf16[6,512,640]{2,0,1:T(8,128)(2,1)} %all-to-all-done) | data formatting | bytes 7864320 | tf_op jit(solution)/shard_map/all_to_all | solution.py:88
  173.9 119.0 %all-to-all-done.1 = bf16[6,512,640]{2,0,1:T(8,128)(2,1)} async-done(((bf16[6,512,640]{2,0,1:T(8,128)(2,1)}), bf16[6,512,640]{2,0,1:T(8,128)(2,1)}, u32[]{:S(2)}, u32[]{:S(2)}) %all-to-all-start.1) | async-done | bytes 3932192 | tf_op jit(solution)/shard_map/all_to_all | solution.py:89
  292.9 8.1 %copy.86 = bf16[6,512,640]{1,2,0:T(8,128)(2,1)} copy(bf16[6,512,640]{2,0,1:T(8,128)(2,1)} %all-to-all-done.1) | data formatting | bytes 7864320 | tf_op jit(solution)/shard_map/all_to_all | solution.py:89
  301.0 19.1 %while.14 = (s32[]{:T(128)}, f32[512,5]{0,1:T(8,128)S(1)}, f32[512,5]{0,1:T(8,128)S(1)}, f32[512,5,128]{0,2,1:T(8,128)S(1)}, s32[]{:T(128)}, /*index=5*/bf16[6,5...) while((s32[]{:T(128)}, f32[512,5]{0,1:T(8,128)S(1)}, ...), condition=%wide.region_8.9_spmd, body=%wide.region_5.8_spmd.sunk | while | flops 682234880 | bytes 20480152 | solution.py:100
  301.7 2.0 bitcast_reduce_fusion.3
  303.7 0.9 fusion.52
  304.6 2.5 fusion.53
  307.8 2.0 bitcast_reduce_fusion.3
  309.8 0.9 fusion.52
  310.7 2.5 fusion.53
  313.9 2.0 bitcast_reduce_fusion.3
  315.9 0.9 fusion.52
  316.8 2.5 fusion.53
  320.1 0.2 divide_convert_fusion
  320.2 163.1 %all-gather.2.cloned.1.call-done = bf16[640,5120]{0,1:T(8,128)(2,1)} async-done(((bf16[640,80]{0,1:T(8,128)(2,1)}), bf16[640,5120]{0,1:T(8,128)(2,1)}) %all-gather.2.cloned.1.call-update) | async-done | bytes 6553616 | tf_op jit(solution)/shard_map/all_gather | solution.py:108
  483.3 0.0 copy-start.1
  483.3 9.1 %convolution_convert_fusion = bf16[512,5120]{1,0:T(8,128)(2,1)} fusion(bf16[512,640]{0,1:T(8,128)(2,1)S(1)} %bitcast.84, bf16[640,5120]{0,1:T(8,128)(2,1)} %all-gather.2.cloned.1.call-done), kind=kOutput, calls=%fused_computation.22 | convolution fusion | flops 3358064640 | bytes 12451840 | tf_op jit(solution)/shard_map/dot_general | solution.py:106
  492.3 0.0 reduce-scatter.2.cloned.1.call-update
  492.4 133.5 %reduce-scatter.2.cloned.1.call-done = bf16[128,5120]{1,0:T(8,128)(2,1)} async-done(((bf16[512,5120]{1,0:T(8,128)(2,1)}), bf16[128,5120]{1,0:T(8,128)(2,1)}) %reduce-scatter.2.cloned.1.call-update) | async-done | bytes 1310736 | tf_op jit(solution)/shard_map/reduce_scatter | solution.py:111
  625.9 0.0 copy-done.1
  (17 shorter events, 0.1 us)
Async XLA Ops:
  6.5 2.4 copy-start
  19.3 12.9 %copy-start.2 = (bf16[128,8,640]{2,1,0:T(8,128)(2,1)S(1)}, bf16[128,8,640]{2,1,0:T(8,128)(2,1)}, u32[]{:S(2)}) copy-start(bf16[128,8,640]{2,1,0:T(8,128)(2,1)} %param.15) | copy-start | bytes 3932164
  19.3 129.1 %all-to-all-start = ((bf16[6,512,640]{2,0,1:T(8,128)(2,1)}), bf16[6,512,640]{2,0,1:T(8,128)(2,1)}, u32[]{:S(2)}, u32[]{:S(2)}) async-start(bf16[6,512,640]{2,0,1:T(8,128)(2,1)} %copy.83), calls=%async_computation | async-start | bytes 10485760 | tf_op jit(solution)/shard_map/all_to_all | solution.py:88
  42.5 115.4 %copy-start.3 = (bf16[1,512,640]{2,1,0:T(8,128)(2,1)S(1)}, bf16[1,512,640]{2,1,0:T(8,128)(2,1)}, u32[]{:S(2)}) copy-start(bf16[1,512,640]{2,1,0:T(8,128)(2,1)} %param.11) | copy-start | bytes 1966084
  42.5 115.7 %copy-start.4 = (bf16[1,512,640]{2,1,0:T(8,128)(2,1)S(1)}, bf16[1,512,640]{2,1,0:T(8,128)(2,1)}, u32[]{:S(2)}) copy-start(bf16[1,512,640]{2,1,0:T(8,128)(2,1)} %param.12) | copy-start | bytes 1966084
  42.5 115.9 %copy-start.5 = (bf16[1,512,640]{2,1,0:T(8,128)(2,1)S(1)}, bf16[1,512,640]{2,1,0:T(8,128)(2,1)}, u32[]{:S(2)}) copy-start(bf16[1,512,640]{2,1,0:T(8,128)(2,1)} %param.13) | copy-start | bytes 1966084
  148.4 144.5 %all-to-all-start.1 = ((bf16[6,512,640]{2,0,1:T(8,128)(2,1)}), bf16[6,512,640]{2,0,1:T(8,128)(2,1)}, u32[]{:S(2)}, u32[]{:S(2)}) async-start(bf16[6,512,640]{2,0,1:T(8,128)(2,1)} %copy.85), calls=%async_computation.1 | async-start | bytes 10485760 | tf_op jit(solution)/shard_map/all_to_all | solution.py:89
  156.9 326.4 %all-gather.2.cloned.1.call-start = ((), (), s32[]{:S(2)}) async-start(), calls=%async_computation.3 | async-start | bytes 6656000 | tf_op jit(solution)/shard_map/all_gather | solution.py:108
  157.6 468.3 %reduce-scatter.2.cloned.1.call-start = ((), (), s32[]{:S(2)}) async-start(), calls=%async_computation.4 | async-start | bytes 6553600 | tf_op jit(solution)/shard_map/reduce_scatter | solution.py:111
  160.8 4.3 copy-start.6
  483.3 142.6 %copy-start.1 = (bf16[128,8,640]{2,1,0:T(8,128)(2,1)S(1)}, bf16[128,8,640]{2,1,0:T(8,128)(2,1)}, u32[]{:S(2)}) copy-start(bf16[128,8,640]{2,1,0:T(8,128)(2,1)} %param.14) | copy-start | bytes 3932164
Sparse Core Ops, SparseCore 0:
  159.5 323.7 all-gather.1
  492.5 133.3 reduce-scatter.1
where the time goes:
time: 634 us; the launch traced here: 633 us
  waiting for transfers between devices  522 us (82%)
  local copies, waits for them, and re-layouts  40.7 us (6%)
  matrix products  26 us (4%)
  starting transfers between devices  21.6 us (3%)
  between operations  13.6 us (2%)
    all_gather x1, waiting for transfers between devices, local(): lax.all_gather(out_weight, 'fsdp', axis=1, tiled=True)  163 us
    reduce_scatter x1, waiting for transfers between devices, local(): lax.psum_scatter(partial_value.astype(jnp.bfloat16), 'clip', scatter_dime...  134 us
    all_to_all x1, waiting for transfers between devices, local(): lax.all_to_all(sent_values, 'fsdp', split_axis=1, concat_axis=1, tiled=True)  119 us
    all_to_all x1, waiting for transfers between devices, local(): lax.all_to_all(sent_keys, 'fsdp', split_axis=1, concat_axis=1, tiled=True)  106 us
    all_to_all x1, starting transfers between devices, local(): lax.all_to_all(sent_keys, 'fsdp', split_axis=1, concat_axis=1, tiled=True)  12.9 us
  transfers between devices with their start and end apart: 4, of which 4 were waited for; matrix products, arithmetic and copies ran while one was open for 8% of the time, Pallas kernels for 0%

commit v1 on v0

--- a/solution.py
+++ b/solution.py
@@ -103,10 +103,15 @@
     attended = (
         (running_out / running_sum[:, :, None]).astype(jnp.bfloat16).reshape(tokens_here, row_width)
     )
+
+    def row_part(z_in, dim_at):
+        e_now = jnp.stack(lax.axis_size("fsdp") * [z_in], 0)
+        return jnp.concatenate(
+            lax.all_to_all(e_now, axis_name="fsdp", split_axis=0, concat_axis=0), dim_at
+        )
+
     partial_value = jnp.dot(
-        attended,
-        lax.all_gather(out_weight, "fsdp", axis=1, tiled=True),
-        preferred_element_type=jnp.float32,
+        attended, row_part(out_weight, dim_at=1), preferred_element_type=jnp.float32
     )
     own_rows = lax.psum_scatter(
         partial_value.astype(jnp.bfloat16), "clip", scatter_dimension=0, tiled=True

time: 634 us -> 542 us (0.85)
  waiting for transfers between devices: 522 us -> 303 us
  blocking collectives: 0 us -> 127 us
    all_gather x1 -> x0, waiting for transfers between devices: 163 us -> none  [local(): lax.all_gather(out_weight, 'fsdp', axis=1, tiled=True)]
    all_to_all x0 -> x1, blocking collectives: none -> 127 us  [local(): lax.all_to_all(sent_values, 'fsdp', split_axis=1, concat_axis=1, tiled=True)]
    reduce_scatter x1, waiting for transfers between devices: 134 us -> 97 us  [local(): lax.psum_scatter(partial_value.astype(jnp.bfloat16), 'clip', scatter_dime...]
    all_to_all x1, waiting for transfers between devices: 119 us -> 100 us  [row_part(): lax.all_to_all(e_now, axis_name='fsdp', split_axis=0, concat_axis=0)]
  transfers between devices with their start and end apart: 4 -> 3, of which waited for: 4 -> 3; matrix products, arithmetic and copies ran while one was open for 8% -> 9% of each run, Pallas kernels for 0% -> 0%
where the time goes in v1:
time: 542 us; the launch traced here: 541 us
  waiting for transfers between devices  303 us (56%)
  blocking collectives  127 us (23%)
  local copies, waits for them, and re-layouts  44.1 us (8%)
  matrix products  26 us (5%)
  starting transfers between devices  19.2 us (4%)
  between operations  13.6 us (3%)
  other arithmetic  5.64 us (1%)
    all_to_all x1, blocking collectives, local(): lax.all_to_all(sent_values, 'fsdp', split_axis=1, concat_axis=1, tiled=True)  127 us
    all_to_all x1, waiting for transfers between devices, local(): lax.all_to_all(sent_keys, 'fsdp', split_axis=1, concat_axis=1, tiled=True)  106 us
    all_to_all x1, waiting for transfers between devices, row_part(): lax.all_to_all(e_now, axis_name='fsdp', split_axis=0, concat_axis=0)  100 us
    reduce_scatter x1, waiting for transfers between devices, local(): lax.psum_scatter(partial_value.astype(jnp.bfloat16), 'clip', scatter_dime...  97 us
    all_to_all x1, starting transfers between devices, local(): lax.all_to_all(sent_keys, 'fsdp', split_axis=1, concat_axis=1, tiled=True)  12.9 us
  transfers between devices with their start and end apart: 3, of which 3 were waited for; matrix products, arithmetic and copies ran while one was open for 9% of the time, Pallas kernels for 0%

profile of v1, /device:TPU:1, one launch (start us, length us, event | category | flops | bytes accessed | tf_op | source)
XLA Modules:
  0.0 540.7 jit_solution(5276696983144412220)
XLA Ops:
  6.5 0.0 copy-start
  6.5 0.9 copy.83
  7.4 0.1 reshape.118
  7.6 0.3 select_reduce_fusion
  7.9 0.9 select_reduce_fusion.1
  8.8 0.1 reshape.128
  8.9 0.0 copy-done
  8.9 3.6 gather_fusion
  12.5 6.8 %copy.84 = bf16[6,512,640]{2,0,1:T(8,128)(2,1)} copy(bf16[6,512,640]{2,1,0:T(8,128)(2,1)} %bitcast.80) | data formatting | bytes 7864320 | tf_op jit(solution)/shard_map/reshape | solution.py:30
  19.3 0.0 copy-start.2
  19.3 12.9 %all-to-all-start = ((bf16[6,512,640]{2,0,1:T(8,128)(2,1)}), bf16[6,512,640]{2,0,1:T(8,128)(2,1)}, u32[]{:S(2)}, u32[]{:S(2)}) async-start(bf16[6,512,640]{2,0,1:T(8,128)(2,1)} %copy.84), calls=%async_computation | async-start | bytes 10485760 | tf_op jit(solution)/shard_map/all_to_all | solution.py:88
  32.2 0.0 copy-done.2
  32.2 3.5 gather_fusion.1
  35.7 6.8 %copy.86 = bf16[6,512,640]{2,0,1:T(8,128)(2,1)} copy(bf16[6,512,640]{2,1,0:T(8,128)(2,1)} %bitcast.79) | data formatting | bytes 7864320 | tf_op jit(solution)/shard_map/reshape | solution.py:31
  42.6 0.0 copy-start.6
  42.6 105.8 %all-to-all-done = bf16[6,512,640]{2,0,1:T(8,128)(2,1)} async-done(((bf16[6,512,640]{2,0,1:T(8,128)(2,1)}), bf16[6,512,640]{2,0,1:T(8,128)(2,1)}, u32[]{:S(2)}, u32[]{:S(2)}) %all-to-all-start) | async-done | bytes 3932192 | tf_op jit(solution)/shard_map/all_to_all | solution.py:88
  148.4 126.5 %all_to_all.15 = bf16[6,512,640]{2,0,1:T(8,128)(2,1)} all-to-all(bf16[6,512,640]{2,0,1:T(8,128)(2,1)} %copy.86), channel_id=1, replica_groups=mesh['clip'=4,'fsdp'=64] {'fsdp'}, dimensions={1} | all-to-all | bytes 7864320 | tf_op jit(solution)/shard_map/all_to_all | solution.py:89
  274.9 0.0 copy-done.6
  274.9 3.2 stack.2
  278.1 0.0 copy-start.3
  278.1 0.0 copy-start.4
  278.1 0.0 copy-start.5
  278.1 6.0 %all-to-all-start.2 = ((bf16[64,640,80]{1,2,0:T(8,128)(2,1)}), bf16[64,640,80]{1,2,0:T(8,128)(2,1)}, u32[]{:S(2)}, u32[]{:S(2)}) async-start(bf16[64,640,80]{1,2,0:T(8,128)(2,1)} %stack.2), calls=%async_computation.2 | async-start | bytes 13107200 | tf_op jit(solution)/shard_map/all_to_all | solution.py:110
  284.2 0.2 reduce-scatter.2.cloned.1.call-start
  284.4 0.0 copy-done.3
  284.4 0.3 copy.77
  284.7 0.0 copy-done.4
  284.7 0.3 copy.76
  285.0 0.0 copy-done.5
  285.0 0.3 copy.80
  285.2 0.3 copy.90
  285.6 0.9 bitcast_reduce_fusion.1
  286.5 0.9 fusion.23
  287.4 0.0 copy-start.7
  287.4 2.5 fusion.31
  289.9 1.7 copy.88
  291.7 0.0 copy-done.7
  291.7 0.7 fusion.35
  292.4 8.1 %copy.85 = bf16[6,512,640]{1,2,0:T(8,128)(2,1)} copy(bf16[6,512,640]{2,0,1:T(8,128)(2,1)} %all-to-all-done) | data formatting | bytes 7864320 | tf_op jit(solution)/shard_map/all_to_all | solution.py:88
  300.4 8.1 %copy.87 = bf16[6,512,640]{1,2,0:T(8,128)(2,1)} copy(bf16[6,512,640]{2,0,1:T(8,128)(2,1)} %all_to_all.15) | data formatting | bytes 7864320 | tf_op jit(solution)/shard_map/all_to_all | solution.py:89
  308.6 19.0 %while.14 = (s32[]{:T(128)}, f32[512,5]{0,1:T(8,128)S(1)}, f32[512,5]{0,1:T(8,128)S(1)}, f32[512,5,128]{0,2,1:T(8,128)S(1)}, s32[]{:T(128)}, /*index=5*/bf16[6,5...) while((s32[]{:T(128)}, f32[512,5]{0,1:T(8,128)S(1)}, ...), condition=%wide.region_8.9_spmd, body=%wide.region_5.8_spmd.sunk | while | flops 682234880 | bytes 20480152 | solution.py:100
  309.3 2.0 bitcast_reduce_fusion.3
  311.3 0.9 fusion.52
  312.2 2.5 fusion.53
  315.4 2.0 bitcast_reduce_fusion.3
  317.4 0.9 fusion.52
  318.3 2.5 fusion.53
  321.5 2.0 bitcast_reduce_fusion.3
  323.5 0.9 fusion.52
  324.4 2.5 fusion.53
  327.6 0.2 divide_convert_fusion
  327.8 100.0 %all-to-all-done.2 = bf16[64,640,80]{1,2,0:T(8,128)(2,1)} async-done(((bf16[64,640,80]{1,2,0:T(8,128)(2,1)}), bf16[64,640,80]{1,2,0:T(8,128)(2,1)}, u32[]{:S(2)}, u32[]{:S(2)}) %all-to-all-start.2) | async-done | bytes 6553632 | tf_op jit(solution)/shard_map/all_to_all | solution.py:110
  427.8 0.0 copy-start.1
  427.8 9.1 %convolution_convert_fusion = bf16[512,5120]{1,0:T(8,128)(2,1)} fusion(bf16[512,640]{0,1:T(8,128)(2,1)S(1)} %bitcast.87, bf16[640,5120]{0,1:T(8,128)(2,1)} %bitcast.16), kind=kOutput, calls=%fused_computation.22 | convolution fusion | flops 3358064640 | bytes 12451840 | tf_op jit(solution)/shard_map/dot_general | solution.py:113
  436.8 0.0 reduce-scatter.2.cloned.1.call-update
  436.9 97.0 %reduce-scatter.2.cloned.1.call-done = bf16[128,5120]{1,0:T(8,128)(2,1)} async-done(((bf16[512,5120]{1,0:T(8,128)(2,1)}), bf16[128,5120]{1,0:T(8,128)(2,1)}) %reduce-scatter.2.cloned.1.call-update) | async-done | bytes 1310736 | tf_op jit(solution)/shard_map/reduce_scatter | solution.py:116
  533.9 0.0 copy-done.1
  (17 shorter events, 0.1 us)
Async XLA Ops:
  6.5 2.4 copy-start
  19.3 12.9 %copy-start.2 = (bf16[128,8,640]{2,1,0:T(8,128)(2,1)S(1)}, bf16[128,8,640]{2,1,0:T(8,128)(2,1)}, u32[]{:S(2)}) copy-start(bf16[128,8,640]{2,1,0:T(8,128)(2,1)} %param.15) | copy-start | bytes 3932164
  19.3 129.1 %all-to-all-start = ((bf16[6,512,640]{2,0,1:T(8,128)(2,1)}), bf16[6,512,640]{2,0,1:T(8,128)(2,1)}, u32[]{:S(2)}, u32[]{:S(2)}) async-start(bf16[6,512,640]{2,0,1:T(8,128)(2,1)} %copy.84), calls=%async_computation | async-start | bytes 10485760 | tf_op jit(solution)/shard_map/all_to_all | solution.py:88
  42.6 232.3 %copy-start.6 = (bf16[640,80]{0,1:T(8,128)(2,1)S(1)}, bf16[640,80]{0,1:T(8,128)(2,1)}, u32[]{:S(2)}) copy-start(bf16[640,80]{0,1:T(8,128)(2,1)} %param.19) | copy-start | bytes 307204
  278.1 6.3 %copy-start.3 = (bf16[1,512,640]{2,1,0:T(8,128)(2,1)S(1)}, bf16[1,512,640]{2,1,0:T(8,128)(2,1)}, u32[]{:S(2)}) copy-start(bf16[1,512,640]{2,1,0:T(8,128)(2,1)} %param.11) | copy-start | bytes 1966084
  278.1 6.6 %copy-start.4 = (bf16[1,512,640]{2,1,0:T(8,128)(2,1)S(1)}, bf16[1,512,640]{2,1,0:T(8,128)(2,1)}, u32[]{:S(2)}) copy-start(bf16[1,512,640]{2,1,0:T(8,128)(2,1)} %param.12) | copy-start | bytes 1966084
  278.1 6.8 %copy-start.5 = (bf16[1,512,640]{2,1,0:T(8,128)(2,1)S(1)}, bf16[1,512,640]{2,1,0:T(8,128)(2,1)}, u32[]{:S(2)}) copy-start(bf16[1,512,640]{2,1,0:T(8,128)(2,1)} %param.13) | copy-start | bytes 1966084
  278.1 149.6 %all-to-all-start.2 = ((bf16[64,640,80]{1,2,0:T(8,128)(2,1)}), bf16[64,640,80]{1,2,0:T(8,128)(2,1)}, u32[]{:S(2)}, u32[]{:S(2)}) async-start(bf16[64,640,80]{1,2,0:T(8,128)(2,1)} %stack.2), calls=%async_computation.2 | async-start | bytes 13107200 | tf_op jit(solution)/shard_map/all_to_all | solution.py:110
  284.2 249.7 %reduce-scatter.2.cloned.1.call-start = ((), (), s32[]{:S(2)}) async-start(), calls=%async_computation.4 | async-start | bytes 6553600 | tf_op jit(solution)/shard_map/reduce_scatter | solution.py:116
  287.4 4.3 copy-start.7
  427.8 106.1 %copy-start.1 = (bf16[128,8,640]{2,1,0:T(8,128)(2,1)S(1)}, bf16[128,8,640]{2,1,0:T(8,128)(2,1)}, u32[]{:S(2)}) copy-start(bf16[128,8,640]{2,1,0:T(8,128)(2,1)} %param.14) | copy-start | bytes 3932164
Sparse Core Ops, SparseCore 0:
  437.0 96.8 reduce-scatter.1
